TPU v7x, 256 devices: a whole 4x4x8 slice. The times are simulated.
256 devices in a mesh: grp: 32 (over x, z), shard: 8 (over y, core).
Axes of the slice: x: 4, y: 4, z: 8, core: 2. Of those that a mesh axis runs over, the one named last changes fastest.
Arguments:
- layer_inputs: bfloat16 [131072, 1600], P(('grp', 'shard')), may hold values from -6 to 6
- cotangents: bfloat16 [131072, 1600], P(('grp', 'shard')), may hold values from -0.25 to 0.25
- weight: bfloat16 [1600, 1600], P('shard'), may hold values from -0.15625 to 0.15625
- error_state: float32 [32, 1600, 1600], P('grp', 'shard'), may hold values from -6 to 6
- momentum: float32 [1600, 1600], P('shard'), may hold values from -0.75 to 0.75
- bias_momentum: float32 [1600], replicated, may hold values from -6 to 6
- start_basis: float32 [1600, 32], replicated, may hold values from -6 to 6
- next_inputs: bfloat16 [131072, 1600], P(('grp', 'shard')), may hold values from -6 to 6
Outputs:
- next_outputs: bfloat16 [131072, 1600], P(('grp', 'shard'))
- new_error: float32 [32, 1600, 1600], P('grp', 'shard')
- new_momentum: float32 [1600, 1600], P('shard')
- new_bias_momentum: float32 [1600], replicated
All inputs are finite; a program needn't handle non-finite values.
Results may differ from a plain program's by a relative error of at most 0.015.
Values may be sent and summed in bfloat16 or wider, within the bound.
No kernel may reach another device: no remote copies, remote signals or barrier semaphores. Data moves between devices by JAX's collectives and lax.ppermute only.
A program may use at most 128 MiB of HBM per device.

v0:
```python
import jax
import jax.numpy as jnp
from jax import lax
from jax.sharding import PartitionSpec as P

momentum_decay = 0.9
learn_rate = 0.1


def shards(
    layer_inputs, cotangents, weight, error_state, momentum, bias_momentum, start_basis, next_inputs
):
    highest = lax.Precision.HIGHEST
    group_count = lax.axis_size("grp")
    rank = start_basis.shape[1]
    gradient = lax.psum_scatter(
        lax.dot_general(
            layer_inputs, cotangents, (((0,), (0,)), ((), ())), preferred_element_type=jnp.float32
        ).astype(jnp.bfloat16),
        "shard",
        scatter_dimension=0,
        tiled=True,
    ).astype(jnp.float32)
    column_sums = jnp.sum(cotangents, axis=0, dtype=jnp.float32)
    corrected = gradient + error_state[0]
    summed = lax.psum(jnp.concatenate([corrected, column_sums[None, :]], axis=0), "grp")
    total = summed[:-1]
    grp_sums = summed[-1]
    basis = start_basis
    ortho = start_basis
    for round_index in range(2):
        factor = jnp.dot(total, basis, precision=highest)
        gram_part = jnp.dot(factor.T, factor, precision=highest)
        if round_index == 0:
            packed = lax.psum(jnp.concatenate([gram_part.reshape(-1), grp_sums]), "shard")
            gram = packed[: rank * rank].reshape(rank, rank)
            all_sums = packed[rank * rank :]
        else:
            gram = lax.psum(gram_part, "shard")
        lower_factor = jnp.linalg.cholesky(gram)
        ortho = jax.scipy.linalg.solve_triangular(lower_factor, factor.T, lower=True).T
        partial_basis = lax.dot_general(total, ortho, (((0,), (0,)), ((), ())), precision=highest)
        basis = lax.psum(partial_basis, "shard") / group_count
    approx = jnp.dot(ortho, basis.T, precision=highest)
    new_error = (corrected - approx)[None, :, :]
    new_momentum = momentum_decay * momentum + approx
    new_bias_momentum = momentum_decay * bias_momentum + all_sums / group_count
    new_weight = (weight.astype(jnp.float32) - learn_rate * new_momentum).astype(jnp.bfloat16)
    projected = jnp.dot(
        next_inputs,
        lax.all_gather(new_weight, "shard", axis=0, tiled=True),
        preferred_element_type=jnp.float32,
    )
    return (projected.astype(jnp.bfloat16), new_error, new_momentum, new_bias_momentum)


def solution(mesh):
    placed = (
        P(("grp", "shard"), None),
        P(("grp", "shard"), None),
        P("shard", None),
        P("grp", "shard", None),
        P("shard", None),
        P(),
        P(),
        P(("grp", "shard"), None),
    )
    return jax.shard_map(
        shards,
        mesh=mesh,
        in_specs=placed,
        out_specs=(P(("grp", "shard"), None), P("grp", "shard", None), P("shard", None), P()),
        check_vma=False,
    )
```

profile of v0, /device:TPU:1, one launch (start us, length us, event | category | flops | bytes accessed | tf_op | source)
XLA Modules:
  0.0 473.4 jit_solution(3598170805652788617)
XLA Ops:
  7.2 1.4 copy-done
  8.6 6.3 %convolution_convert_fusion = bf16[1600,1600]{1,0:T(8,128)(2,1)} fusion(bf16[512,1600]{0,1:T(8,128)(2,1)S(1)} %copy-done, bf16[512,1600]{0,1:T(8,128)(2,1)} %param.12), kind=kOutput, calls=%fused_computation | convolution fusion | flops 2624000000 | bytes 8396800 | tf_op jit(solution)/shard_map/dot_general | solution.py:17
  15.0 1.4 copy-done.3
  16.7 48.7 %reduce-scatter.4.cloned.1.call-done = bf16[200,1600]{1,0:T(8,128)(2,1)} async-done(((bf16[1600,1600]{1,0:T(8,128)(2,1)}), bf16[200,1600]{1,0:T(8,128)(2,1)}) %reduce-scatter.4.cloned.1.call-update) | async-done | bytes 640016
  65.4 1.6 bitcast_add_fusion
  67.0 1.1 copy-done.2
  68.1 1.2 pad_maximum_fusion
  69.3 149.4 %all-reduce.5.cloned.1.call-done = f32[201,1600]{1,0:T(8,128)} async-done(((f32[201,1600]{1,0:T(8,128)}), f32[201,1600]{1,0:T(8,128)}) %all-reduce.5.cloned.1.call-update) | async-done | bytes 1286416 | tf_op jit(solution)/shard_map/psum | solution.py:26
  218.7 2.8 fusion.7
  221.8 25.7 %psum.36 = f32[2624]{0:T(1024)S(1)} all-reduce(f32[2624]{0:T(1024)S(1)} %pad_maximum_fusion.1), channel_id=1, replica_groups=mesh['grp'=32,'shard'=8] {'shard'}, use_global_device_ids=true, to_apply=%region_3.0 | all-reduce | flops 2624 | bytes 20992 | tf_op jit(solution)/shard_map/psum | solution.py:35
  247.7 2.9 cholesky.44
  251.3 0.7 fusion.18
  251.9 2.4 custom-call.6
  254.6 1.7 fusion.5
  256.4 60.6 %all-reduce.7.cloned.1.call-done = f32[1600,32]{0,1:T(8,128)} async-done(((f32[1600,32]{0,1:T(8,128)}), f32[1600,32]{0,1:T(8,128)}) %all-reduce.7.cloned.1.call-update) | async-done | bytes 204816 | tf_op jit(solution)/shard_map/psum | solution.py:43
  317.0 2.3 fusion.3
  319.4 21.9 %psum.38 = f32[32,32]{0,1:T(8,128)S(1)} all-reduce(f32[32,32]{0,1:T(8,128)S(1)} %fusion.32), channel_id=1, replica_groups=mesh['grp'=32,'shard'=8] {'shard'}, use_global_device_ids=true, to_apply=%region_7.10 | all-reduce | flops 1024 | bytes 8192 | tf_op jit(solution)/shard_map/psum | solution.py:39
  341.4 2.9 cholesky.55
  345.7 2.4 custom-call.7
  348.3 1.7 fusion.1
  350.1 64.9 %all-reduce.9.cloned.1.call-done = f32[1600,32]{0,1:T(8,128)} async-done(((f32[1600,32]{0,1:T(8,128)}), f32[1600,32]{0,1:T(8,128)}) %all-reduce.9.cloned.1.call-update) | async-done | bytes 204816 | tf_op jit(solution)/shard_map/psum | solution.py:43
  415.0 5.2 %subtract_convert_fusion = (bf16[200,1600]{1,0:T(8,128)(2,1)}, f32[200,1600]{1,0:T(8,128)}, f32[1,200,1600]{2,1,0:T(8,128)}) fusion(bf16[200,1600]{1,0:T(8,128)(2,1)} %param.13, f32[200,1600]{1,0:T(8,128)} %param.15, f32[200,1600]{1,0:T(8,128)} %copy-done.2, f32[32,200]{1,0:T(8,128)S(1)} %fusion.14, f32[1600,32]{0,1:T(8,128)} %all-reduce.9.cloned.1.call-done), kind=kOutput, calls=%fused_computation.7 | convolution fusion | flops 125171200 | bytes 6630400 | tf_op jit(solution)/shard_map/dot_general | solution.py:44
  420.8 38.7 %all-gather.2.cloned.1.call-done = bf16[1600,1600]{1,0:T(8,128)(2,1)} async-done(((bf16[200,1600]{1,0:T(8,128)(2,1)}), bf16[1600,1600]{1,0:T(8,128)(2,1)}) %all-gather.2.cloned.1.call-update) | async-done | bytes 5120016 | tf_op jit(solution)/shard_map/all_gather | solution.py:51
  459.5 7.4 %fusion = bf16[512,1600]{0,1:T(8,128)(2,1)} fusion(bf16[1600,1600]{1,0:T(8,128)(2,1)} %all-gather.2.cloned.1.call-done, bf16[512,1600]{0,1:T(8,128)(2,1)} %param.18), kind=kOutput, calls=%fused_computation.3 | convolution fusion | flops 2622259200 | bytes 8396800 | tf_op jit(solution)/shard_map/dot_general | solution.py:49
  (40 shorter events, 4.4 us)
Async XLA Ops:
  7.2 1.4 copy-start
  7.2 58.2 %reduce-scatter.4.cloned.1.call-start = ((), (), s32[]{:S(2)}) async-start(), calls=%async_computation.5 | async-start | bytes 5990400
  14.9 1.4 copy-start.3
  14.9 203.7 %all-reduce.5.cloned.1.call-start = ((), (), s32[]{:S(2)}) async-start(), calls=%async_computation.1 | async-start | bytes 2768896 | tf_op jit(solution)/shard_map/psum | solution.py:26
  67.0 1.1 copy-start.2
  68.1 150.6 %copy-start.4 = (f32[1600,32]{0,1:T(8,128)S(1)}, f32[1600,32]{0,1:T(8,128)}, u32[]{:S(2)}) copy-start(f32[1600,32]{0,1:T(8,128)} %param.17) | copy-start | bytes 614404
  69.3 247.7 %all-reduce.7.cloned.1.call-start = ((), (), s32[]{:S(2)}) async-start(), calls=%async_computation.2 | async-start | bytes 425984 | tf_op jit(solution)/shard_map/psum | solution.py:43
  218.7 3.0 copy-start.1
  256.3 158.7 %all-reduce.9.cloned.1.call-start = ((), (), s32[]{:S(2)}) async-start(), calls=%async_computation.3 | async-start | bytes 425984 | tf_op jit(solution)/shard_map/psum | solution.py:43
  350.0 70.2 %copy-start.5 = (f32[1600]{0:T(1024)S(1)}, f32[1600]{0:T(1024)}, u32[]{:S(2)}) copy-start(f32[1600]{0:T(1024)} %param.16) | copy-start | bytes 19204
  350.0 109.5 %all-gather.2.cloned.1.call-start = ((), (), s32[]{:S(2)}) async-start(), calls=%async_computation.4 | async-start | bytes 5990400 | tf_op jit(solution)/shard_map/all_gather | solution.py:51
Sparse Core Ops, SparseCore 0:
  15.1 50.2 reduce-scatter.3
  69.4 149.1 all-reduce.4
  256.4 60.4 all-reduce.6
  350.1 64.7 all-reduce.8
  420.3 39.1 all-gather.1
where the time goes:
time: 474 us; the launch traced here: 473 us
  waiting for transfers between devices  362 us (76%)
  blocking collectives  47.7 us (10%)
  matrix products  28.1 us (6%)
  other arithmetic  17.1 us (4%)
  between operations  13.9 us (3%)
    psum x1, waiting for transfers between devices, shards(): lax.psum(jnp.concatenate([corrected, column_sums[None, :]], axis=0), 'grp')  149 us
    psum x2, waiting for transfers between devices, shards(): basis = lax.psum(partial_basis, 'shard') / group_count  125 us
    unnamed x6, waiting for transfers between devices  48.8 us
    all_gather x1, waiting for transfers between devices, shards(): lax.all_gather(new_weight, 'shard', axis=0, tiled=True)  38.7 us
    psum x1, blocking collectives, shards(): lax.psum(jnp.concatenate([gram_part.reshape(-1), grp_sums]), 'shard')  25.7 us
    psum x1, blocking collectives, shards(): gram = lax.psum(gram_part, 'shard')  21.9 us
  transfers between devices with their start and end apart: 5, of which 5 were waited for; matrix products, arithmetic and copies ran while one was open for 0% of the time, Pallas kernels for 0%

commit v1 on v0

--- a/solution.py
+++ b/solution.py
@@ -40,7 +40,7 @@
         lower_factor = jnp.linalg.cholesky(gram)
         ortho = jax.scipy.linalg.solve_triangular(lower_factor, factor.T, lower=True).T
         partial_basis = lax.dot_general(total, ortho, (((0,), (0,)), ((), ())), precision=highest)
-        basis = lax.psum(partial_basis, "shard") / group_count
+        basis = jnp.sum(lax.all_gather(partial_basis, "shard"), axis=0) / group_count
     approx = jnp.dot(ortho, basis.T, precision=highest)
     new_error = (corrected - approx)[None, :, :]
     new_momentum = momentum_decay * momentum + approx

time: 474 us -> 404 us (0.85)
  waiting for transfers between devices: 362 us -> 291 us
    psum x2 -> x0, waiting for transfers between devices: 125 us -> none  [shards(): basis = lax.psum(partial_basis, 'shard') / group_count]
    all_gather x0 -> x2, waiting for transfers between devices: none -> 54.1 us  [shards(): lax.all_gather(partial_basis, 'shard')]
where the time goes in v1:
time: 404 us; the launch traced here: 403 us
  waiting for transfers between devices  291 us (72%)
  blocking collectives  46.8 us (12%)
  matrix products  26.7 us (7%)
  other arithmetic  20.2 us (5%)
  between operations  13.9 us (3%)
  local copies, waits for them, and re-layouts  4.13 us (1%)
    psum x1, waiting for transfers between devices, shards(): lax.psum(jnp.concatenate([corrected, column_sums[None, :]], axis=0), 'grp')  149 us
    all_gather x2, waiting for transfers between devices, shards(): lax.all_gather(partial_basis, 'shard')  54.1 us
    unnamed x6, waiting for transfers between devices  48.8 us
    all_gather x1, waiting for transfers between devices, shards(): lax.all_gather(new_weight, 'shard', axis=0, tiled=True)  39.2 us
    psum x1, blocking collectives, shards(): lax.psum(jnp.concatenate([gram_part.reshape(-1), grp_sums]), 'shard')  25.7 us
    psum x1, blocking collectives, shards(): gram = lax.psum(gram_part, 'shard')  21.1 us
  transfers between devices with their start and end apart: 5, of which 5 were waited for; matrix products, arithmetic and copies ran while one was open for 0% of the time, Pallas kernels for 0%

profile of v1, /device:TPU:1, one launch (start us, length us, event | category | flops | bytes accessed | tf_op | source)
XLA Modules:
  0.0 403.5 jit_solution(14824272835183960789)
XLA Ops:
  7.2 1.4 copy-done
  8.6 6.3 %convolution_convert_fusion = bf16[1600,1600]{1,0:T(8,128)(2,1)} fusion(bf16[512,1600]{0,1:T(8,128)(2,1)S(1)} %copy-done, bf16[512,1600]{0,1:T(8,128)(2,1)} %param.12), kind=kOutput, calls=%fused_computation | convolution fusion | flops 2624000000 | bytes 8396800 | tf_op jit(solution)/shard_map/dot_general | solution.py:17
  15.0 1.4 copy-done.4
  16.7 48.7 %reduce-scatter.4.cloned.1.call-done = bf16[200,1600]{1,0:T(8,128)(2,1)} async-done(((bf16[1600,1600]{1,0:T(8,128)(2,1)}), bf16[200,1600]{1,0:T(8,128)(2,1)}) %reduce-scatter.4.cloned.1.call-update) | async-done | bytes 640016
  65.4 1.6 bitcast_add_fusion
  68.1 1.2 pad_maximum_fusion
  69.3 149.4 %all-reduce.3.cloned.1.call-done = f32[201,1600]{1,0:T(8,128)} async-done(((f32[201,1600]{1,0:T(8,128)}), f32[201,1600]{1,0:T(8,128)}) %all-reduce.3.cloned.1.call-update) | async-done | bytes 1286416 | tf_op jit(solution)/shard_map/psum | solution.py:26
  218.7 2.8 fusion.5
  221.8 25.7 %psum.22 = f32[2624]{0:T(1024)S(1)} all-reduce(f32[2624]{0:T(1024)S(1)} %pad_maximum_fusion.1), channel_id=1, replica_groups=mesh['grp'=32,'shard'=8] {'shard'}, use_global_device_ids=true, to_apply=%region_3.0 | all-reduce | flops 2624 | bytes 20992 | tf_op jit(solution)/shard_map/psum | solution.py:35
  247.7 2.9 cholesky.44
  251.9 2.4 custom-call.6
  254.6 1.7 convolution_bitcast_fusion.1
  256.4 24.8 %all-gather.10.cloned.1.call-done = f32[8,1600,32]{1,2,0:T(8,128)} async-done(((f32[1,1600,32]{1,2,0:T(8,128)}), f32[8,1600,32]{1,2,0:T(8,128)}) %all-gather.10.cloned.1.call-update) | async-done | bytes 1638416 | tf_op jit(solution)/shard_map/all_gather | solution.py:43
  281.2 1.6 reduce_sum.28
  282.7 1.4 fusion.2
  284.3 21.1 %psum.23 = f32[32,32]{0,1:T(8,128)S(1)} all-reduce(f32[32,32]{0,1:T(8,128)S(1)} %fusion.30), channel_id=1, replica_groups=mesh['grp'=32,'shard'=8] {'shard'}, use_global_device_ids=true, to_apply=%region_7.10 | all-reduce | flops 1024 | bytes 8192 | tf_op jit(solution)/shard_map/psum | solution.py:39
  305.4 2.9 cholesky.55
  309.7 2.4 custom-call.7
  312.4 1.7 convolution_bitcast_fusion
  314.1 29.4 %all-gather.12.cloned.1.call-done = f32[8,1600,32]{1,2,0:T(8,128)} async-done(((f32[1,1600,32]{1,2,0:T(8,128)}), f32[8,1600,32]{1,2,0:T(8,128)}) %all-gather.12.cloned.1.call-update) | async-done | bytes 1638416 | tf_op jit(solution)/shard_map/all_gather | solution.py:43
  343.5 1.6 reduce_sum.29
  345.0 4.7 %subtract_convert_fusion = (bf16[200,1600]{1,0:T(8,128)(2,1)}, f32[200,1600]{1,0:T(8,128)}, f32[1,200,1600]{2,1,0:T(8,128)}) fusion(bf16[200,1600]{1,0:T(8,128)(2,1)} %param.13, f32[200,1600]{1,0:T(8,128)} %param.15, f32[200,1600]{1,0:T(8,128)S(1)} %copy-done.3, f32[32,200]{1,0:T(8,128)S(1)} %fusion.12, f32[1600,32]{0,1:T(8,128)S(1)} %reduce_sum.29), kind=kOutput, calls=%fused_computation.9 | convolution fusion | flops 125171200 | bytes 6630400 | tf_op jit(solution)/shard_map/dot_general | solution.py:44
  350.4 39.2 %all-gather.8.cloned.1.call-done = bf16[1600,1600]{1,0:T(8,128)(2,1)} async-done(((bf16[200,1600]{1,0:T(8,128)(2,1)}), bf16[1600,1600]{1,0:T(8,128)(2,1)}) %all-gather.8.cloned.1.call-update) | async-done | bytes 5120016 | tf_op jit(solution)/shard_map/all_gather | solution.py:51
  389.6 7.4 %fusion = bf16[512,1600]{0,1:T(8,128)(2,1)} fusion(bf16[1600,1600]{1,0:T(8,128)(2,1)} %all-gather.8.cloned.1.call-done, bf16[512,1600]{0,1:T(8,128)(2,1)} %param.18), kind=kOutput, calls=%fused_computation.3 | convolution fusion | flops 2622259200 | bytes 8396800 | tf_op jit(solution)/shard_map/dot_general | solution.py:49
  (44 shorter events, 6.1 us)
Async XLA Ops:
  7.2 1.4 copy-start
  7.2 58.2 %reduce-scatter.4.cloned.1.call-start = ((), (), s32[]{:S(2)}) async-start(), calls=%async_computation.5 | async-start | bytes 5990400
  14.9 1.4 copy-start.4
  14.9 203.7 %all-reduce.3.cloned.1.call-start = ((), (), s32[]{:S(2)}) async-start(), calls=%async_computation.1 | async-start | bytes 2768896 | tf_op jit(solution)/shard_map/psum | solution.py:26
  67.0 1.1 copy-start.2
  68.1 150.6 %copy-start.5 = (f32[1600,32]{0,1:T(8,128)S(1)}, f32[1600,32]{0,1:T(8,128)}, u32[]{:S(2)}) copy-start(f32[1600,32]{0,1:T(8,128)} %param.17) | copy-start | bytes 614404
  69.3 211.9 %all-gather.10.cloned.1.call-start = ((), (), s32[]{:S(2)}) async-start(), calls=%async_computation.3 | async-start | bytes 1916928 | tf_op jit(solution)/shard_map/all_gather | solution.py:43
  218.7 3.0 copy-start.1
  256.3 87.1 %all-gather.12.cloned.1.call-start = ((), (), s32[]{:S(2)}) async-start(), calls=%async_computation.4 | async-start | bytes 1916928 | tf_op jit(solution)/shard_map/all_gather | solution.py:43
  314.0 31.0 %copy-start.3 = (f32[200,1600]{1,0:T(8,128)S(1)}, f32[200,1600]{1,0:T(8,128)}, u32[]{:S(2)}) copy-start(f32[200,1600]{1,0:T(8,128)} %copy-done.2) | copy-start | bytes 3840004
  314.1 75.5 %all-gather.8.cloned.1.call-start = ((), (), s32[]{:S(2)}) async-start(), calls=%async_computation.2 | async-start | bytes 5990400 | tf_op jit(solution)/shard_map/all_gather | solution.py:51
  345.0 4.8 %copy-start.6 = (f32[1600]{0:T(1024)S(1)}, f32[1600]{0:T(1024)}, u32[]{:S(2)}) copy-start(f32[1600]{0:T(1024)} %param.16) | copy-start | bytes 19204
Sparse Core Ops, SparseCore 0:
  15.1 50.2 reduce-scatter.3
  69.4 149.1 all-reduce.2
  256.4 24.6 all-gather.9
  314.2 29.2 all-gather.11
  349.9 39.5 all-gather.7
